TPU v7x, 256 devices: a whole 4x4x8 slice. The times are simulated.
256 devices in a mesh: tm: 16 (over z, core), head: 16 (over y, x).
Axes of the slice: x: 4, y: 4, z: 8, core: 2. Of those that a mesh axis runs over, the one named last changes fastest.
Arguments:
- frames: bfloat16 [8192, 2048], P(('tm', 'head')), may hold values from -6 to 6
- log_decay: float32 [8192, 16], P('tm', 'head'), may hold values from -2 to 0, as said below
- w_query: bfloat16 [2048, 2048], P('tm', 'head'), may hold values from -0.125 to 0.125
- w_key: bfloat16 [2048, 2048], P('tm', 'head'), may hold values from -0.125 to 0.125
- w_value: bfloat16 [2048, 2048], P('tm', 'head'), may hold values from -0.125 to 0.125
- w_gate: bfloat16 [2048, 2048], P('tm', 'head'), may hold values from -0.125 to 0.125
- w_out: bfloat16 [2048, 2048], P('head', 'tm'), may hold values from -0.125 to 0.125
Outputs:
- mixed: bfloat16 [8192, 2048], P(('tm', 'head'))
Inputs may be any that keep to these rules, and one draw needn't show every extreme that they name: `log_decay`: strictly negative.
All inputs are finite; a program needn't handle non-finite values.
Results may differ from a plain program's by a relative error of at most 0.015.
Values may be sent and summed in bfloat16 or wider, within the bound.
No kernel may reach another device: no remote copies, remote signals or barrier semaphores. Data moves between devices by JAX's collectives and lax.ppermute only.
A program may use at most 64 MiB of HBM per device.

v0:
```python
import jax
import jax.numpy as jnp
from jax import lax
from jax.sharding import PartitionSpec as P

HEAD_DIM = 128
BLOCK = 512
PAD_ROWS = 8


def gather_by_exchange(part, axis):
    count = lax.axis_size(axis)
    copies = jnp.broadcast_to(part[None], (count,) + part.shape)
    return lax.all_to_all(copies, axis, 0, 0, tiled=False)


def prior_state(local_final, log_total, axis):
    heads_here = local_final.shape[0]
    high = log_total.astype(jnp.bfloat16)
    low = (log_total - high.astype(jnp.float32)).astype(jnp.bfloat16)
    extra = jnp.concatenate(
        [
            jnp.broadcast_to(high[:, None, None], (heads_here, 1, HEAD_DIM)),
            jnp.broadcast_to(low[:, None, None], (heads_here, 1, HEAD_DIM)),
            jnp.zeros((heads_here, PAD_ROWS - 2, HEAD_DIM), jnp.bfloat16),
        ],
        axis=1,
    )
    packed = jnp.concatenate([local_final.astype(jnp.bfloat16), extra], axis=1)
    gathered = gather_by_exchange(packed, axis)
    finals = gathered[:, :, :HEAD_DIM, :].astype(jnp.float32)
    totals = gathered[:, :, HEAD_DIM, 0].astype(jnp.float32) + gathered[
        :, :, HEAD_DIM + 1, 0
    ].astype(jnp.float32)
    count = gathered.shape[0]
    mine = lax.axis_index(axis)
    order = jnp.arange(count, dtype=jnp.int32)
    between = (order[:, None] < order[None, :]) & (order[None, :] < mine)
    exponent = jnp.sum(jnp.where(between[:, :, None], totals[None, :, :], 0.0), axis=1)
    weight = jnp.where((order < mine)[:, None], jnp.exp(exponent), 0.0)
    return jnp.sum(weight[:, :, None, None] * finals, axis=0)


def shards(frames, log_decay, w_query, w_key, w_value, w_gate, w_out):
    head_width = w_query.shape[1]
    blocks = [w_query, w_key, w_value, w_gate, w_out]
    width = sum((block.shape[1] for block in blocks))
    column = jnp.arange(width)[None, :]
    packed = jnp.pad(blocks[-1], ((0, 0), (width - head_width, 0)))
    for start, block in reversed(list(zip(range(0, width, head_width), blocks))[:-1]):
        padded = jnp.pad(block, ((0, 0), (start, width - start - head_width)))
        packed = jnp.where(column < start + head_width, padded, packed)
    stacked = lax.all_gather(packed, "tm", axis=0, tiled=True)
    joined = stacked[:, : 4 * head_width]
    out_blocks = stacked[:, 4 * head_width :].reshape(-1, head_width, w_out.shape[1])
    frames_here = gather_by_exchange(frames, "head").reshape(-1, frames.shape[1])
    projected = jnp.dot(frames_here, joined, preferred_element_type=jnp.float32)
    local_len = projected.shape[0]
    heads_here = head_width // HEAD_DIM
    block_count = local_len // BLOCK
    query_blocks = (
        projected[:, :head_width]
        .astype(jnp.bfloat16)
        .reshape(block_count, BLOCK, heads_here, HEAD_DIM)
    )
    key_blocks = (
        projected[:, head_width : 2 * head_width]
        .astype(jnp.bfloat16)
        .reshape(block_count, BLOCK, heads_here, HEAD_DIM)
    )
    value_blocks = (
        projected[:, 2 * head_width : 3 * head_width]
        .astype(jnp.bfloat16)
        .reshape(block_count, BLOCK, heads_here, HEAD_DIM)
    )
    gate_all = projected[:, 3 * head_width :]
    running_blocks = jnp.cumsum(log_decay.reshape(block_count, BLOCK, heads_here), axis=1)
    slice_ordinal = jnp.arange(BLOCK, dtype=jnp.int32)
    causal = slice_ordinal[:, None] >= slice_ordinal[None, :]

    def local_step(carry_state, inputs):
        query_block, key_block, value_block, running = inputs
        gaps = running.T[:, :, None] - running.T[:, None, :]
        decay = jnp.exp(jnp.where(causal[None], gaps, -jnp.inf))
        scores = jnp.einsum(
            "thd,shd->hts", query_block, key_block, preferred_element_type=jnp.float32
        )
        weights = (scores * decay).astype(jnp.bfloat16)
        intra = jnp.einsum("hts,shd->thd", weights, value_block, preferred_element_type=jnp.float32)
        scaled = (
            key_block.astype(jnp.float32) * jnp.exp(running[-1][None, :] - running)[:, :, None]
        ).astype(jnp.bfloat16)
        update = jnp.einsum("shd,she->hde", scaled, value_block, preferred_element_type=jnp.float32)
        next_state = jnp.exp(running[-1])[:, None, None] * carry_state + update
        return (next_state, (intra, carry_state))

    zero_state = jnp.zeros((heads_here, HEAD_DIM, HEAD_DIM), jnp.float32)
    local_final, (intra_all, local_starts) = lax.scan(
        local_step, zero_state, (query_blocks, key_blocks, value_blocks, running_blocks)
    )
    prior = prior_state(local_final, jnp.sum(log_decay, axis=0), "tm")
    block_logs = running_blocks[:, -1, :]
    before = jnp.cumsum(block_logs, axis=0) - block_logs
    start_states = jnp.exp(before)[:, :, None, None] * prior[None] + local_starts
    lifted = query_blocks.astype(jnp.float32) * jnp.exp(running_blocks)[..., None]
    inter = jnp.einsum("cthd,chde->cthe", lifted, start_states, precision=lax.Precision.HIGHEST)
    retained = (intra_all + inter).reshape(local_len, heads_here, HEAD_DIM)
    center = jnp.mean(retained, axis=-1, keepdims=True)
    spread = jnp.mean((retained - center) ** 2, axis=-1, keepdims=True)
    normed = (retained - center) / jnp.sqrt(spread + 1e-05)
    gated = (
        (jax.nn.silu(gate_all.reshape(local_len, heads_here, HEAD_DIM)) * normed)
        .astype(jnp.bfloat16)
        .reshape(local_len, head_width)
    )
    heads = lax.axis_size("head")
    side = int(round(heads**0.5))
    me = lax.axis_index("head")
    row, col = (me // side, me % side)
    rows_mine = out_blocks
    ring_order = sorted(range(1, side), key=lambda shift: -min(shift, side - shift))
    by_owner = gated.reshape(side, side, local_len // heads, head_width)
    units = lax.axis_size("tm")
    half = rows_mine.shape[0] // 2
    parity = lax.axis_index("tm") % 2
    own_half = lax.dynamic_slice_in_dim(rows_mine, parity * half, half, axis=0)
    pieces = [lax.dynamic_index_in_dim(by_owner, col, axis=1, keepdims=False)]
    fetched = []
    for shift in ring_order:
        across = [(h, h // side * side + (h % side + shift) % side) for h in range(heads)]
        piece = lax.dynamic_index_in_dim(by_owner, (col + shift) % side, axis=1, keepdims=False)
        pieces.append(lax.ppermute(piece, "head", across))
        fetched.append(lax.ppermute(own_half, "head", across))
    fetched = jnp.stack(fetched)
    swapped = lax.ppermute(fetched, "tm", [(t, t ^ 1) for t in range(units)])
    first = jnp.where(parity == 0, fetched, swapped)
    second = jnp.where(parity == 0, swapped, fetched)
    remote = jnp.concatenate([first, second], axis=1)
    weights_in = [rows_mine] + [remote[s] for s in range(side - 1)]
    partial = jnp.einsum(
        "syfr,skrc->yfkc",
        jnp.stack(pieces),
        jnp.stack(weights_in),
        preferred_element_type=jnp.float32,
    ).astype(jnp.bfloat16)
    partial = partial.reshape(side, local_len // heads, -1)
    total = lax.dynamic_index_in_dim(partial, row, axis=0, keepdims=False).astype(jnp.float32)
    for shift in ring_order:
        down = [(h, (h // side + shift) % side * side + h % side) for h in range(heads)]
        piece = lax.dynamic_index_in_dim(partial, (row + shift) % side, axis=0, keepdims=False)
        total = total + lax.ppermute(piece, "head", down).astype(jnp.float32)
    return total.astype(jnp.bfloat16)


def solution(mesh):
    return jax.shard_map(
        shards,
        mesh=mesh,
        in_specs=(
            P(("tm", "head"), None),
            P("tm", "head"),
            P("tm", "head"),
            P("tm", "head"),
            P("tm", "head"),
            P("tm", "head"),
            P("head", "tm"),
        ),
        out_specs=P(("tm", "head"), None),
        check_vma=False,
    )
```

profile of v0, /device:TPU:6, one launch (start us, length us, event | category | flops | bytes accessed | tf_op | source)
XLA Modules:
  0.0 110.7 jit_solution(12447846987612990103)
XLA Ops:
  6.5 1.6 %select_select_fusion = bf16[128,640]{1,0:T(8,128)(2,1)} fusion(bf16[128,128]{1,0:T(8,128)(2,1)} %param.13, bf16[128,128]{1,0:T(8,128)(2,1)} %param.12, bf16[128,128]{1,0:T(8,128)(2,1)} %param.11, bf16[128,128]{1,0:T(8,128)(2,1)} %param.10, bf16[128,128]{1,0:T(8,128)(2,1)} %param.9, pred[640]{0:T(1024)(128)(4,1)S(1)} %get-tuple-element.47, ...), kind=kLoop, calls=%fused_computation.47 | loop fusion | flops 327680 | bytes 330240 | tf_op jit(solution)/shard_map/jit(_where)/select_n | solution.py:52
  8.1 2.5 %broadcast_in_dim.113 = bf16[16,32,2048]{2,1,0:T(8,128)(2,1)} broadcast(bf16[32,2048]{1,0:T(8,128)(2,1)} %param.7), dimensions={1,2} | broadcast | bytes 2228224 | tf_op jit(solution)/shard_map/broadcast_in_dim | solution.py:13
  10.6 7.6 %all-to-all-start = ((bf16[16,32,2048]{2,1,0:T(8,128)(2,1)}), bf16[16,32,2048]{2,1,0:T(8,128)(2,1)S(1)}, u32[]{:S(2)}, u32[]{:S(2)}) async-start(bf16[16,32,2048]{2,1,0:T(8,128)(2,1)} %broadcast_in_dim.113), calls=%async_computation | async-start | bytes 4194304 | tf_op jit(solution)/shard_map/all_to_all | solution.py:14
  23.6 22.9 %all-to-all-done = bf16[16,32,2048]{2,1,0:T(8,128)(2,1)S(1)} async-done(((bf16[16,32,2048]{2,1,0:T(8,128)(2,1)}), bf16[16,32,2048]{2,1,0:T(8,128)(2,1)S(1)}, u32[]{:S(2)}, u32[]{:S(2)}) %all-to-all-start) | async-done | bytes 2097184 | tf_op jit(solution)/shard_map/all_to_all | solution.py:14
  46.4 6.1 %all-gather.2.cloned.1.call-done = bf16[2048,640]{1,0:T(8,128)(2,1)} async-done(((bf16[128,640]{1,0:T(8,128)(2,1)}), bf16[2048,640]{1,0:T(8,128)(2,1)}) %all-gather.2.cloned.1.call-update) | async-done | bytes 2621456 | tf_op jit(solution)/shard_map/all_gather | solution.py:53
  52.6 3.8 %fusion.58 = (bf16[512,512]{1,0:T(8,128)(2,1)S(1)}, f32[512,512]{1,0:T(8,128)}) fusion(bf16[512,2048]{1,0:T(8,128)(2,1)S(1)} %bitcast.110, bf16[2048,640]{1,0:T(8,128)(2,1)} %all-gather.2.cloned.1.call-done), kind=kOutput, calls=%fused_computation.95 | convolution fusion | flops 1074003968 | bytes 5767168 | tf_op jit(solution)/shard_map/dot_general | solution.py:57
  56.9 0.9 broadcast_in_dim.122
  57.8 4.0 %all-to-all-start.1 = ((bf16[16,1,136,128]{3,2,1,0:T(8,128)(2,1)}), bf16[16,1,136,128]{3,2,1,0:T(8,128)(2,1)S(1)}, u32[]{:S(2)}, u32[]{:S(2)}) async-start(bf16[16,1,136,128]{3,2,1,0:T(8,128)(2,1)} %broadcast_in_dim.122), calls=%async_computation.1 | async-start | bytes 1114112 | tf_op jit(solution)/shard_map/all_to_all | solution.py:14
  64.4 1.1 slice.73
  65.6 1.5 %collective-permute-start.3 = (bf16[8,128,128]{2,1,0:T(8,128)(2,1)S(1)}, bf16[8,128,128]{2,1,0:T(8,128)(2,1)S(1)}, u32[]{:S(2)}, u32[]{:S(2)}) collective-permute-start(bf16[8,128,128]{2,1,0:T(8,128)(2,1)S(1)} %constant_dynamic-slice_fusion), channel_id=1, source_target_pairs={{0,2},{1,3},{2,0},{3,1},{4,6},{5,7},{6,4},{7,5},{8,10},{9,11},{10,... | collective-permute-start | bytes 786440 | tf_op jit(solution)/shard_map/ppermute | solution.py:133
  67.1 2.4 %collective-permute-start.4 = (bf16[8,128,128]{2,1,0:T(8,128)(2,1)S(1)}, bf16[8,128,128]{2,1,0:T(8,128)(2,1)S(1)}, u32[]{:S(2)}, u32[]{:S(2)}) collective-permute-start(bf16[8,128,128]{2,1,0:T(8,128)(2,1)S(1)} %constant_dynamic-slice_fusion), channel_id=1, source_target_pairs={{0,1},{1,2},{2,3},{3,0},{4,5},{5,6},{6,7},{7,4},{8,9},{9,10},{10,1... | collective-permute-start | bytes 786440 | tf_op jit(solution)/shard_map/ppermute | solution.py:133
  69.5 1.2 %fusion.15 = f32[1,512,1,128]{3,1,2,0:T(8,128)} fusion(f32[512]{0:T(512)S(1)} %get-tuple-element.22, bf16[512,512]{1,0:T(8,128)(2,1)S(1)} %get-tuple-element.43), kind=kOutput, calls=%fused_computation.16 | convolution fusion | flops 135528448 | bytes 659456 | tf_op jit(solution)/shard_map/while/body/eval_jaxpr/hts,shd->thd/dot_general | solution.py:89
  70.7 5.6 %collective-permute-done.3 = bf16[8,128,128]{2,1,0:T(8,128)(2,1)S(1)} collective-permute-done((bf16[8,128,128]{2,1,0:T(8,128)(2,1)S(1)}, bf16[8,128,128]{2,1,0:T(8,128)(2,1)S(1)}, u32[]{:S(2)}, u32[]{:S(2)}) %collective-permute-start.3) | collective-permute-done | bytes 262176 | tf_op jit(solution)/shard_map/ppermute | solution.py:133
  76.3 4.1 %collective-permute-done.4 = bf16[8,128,128]{2,1,0:T(8,128)(2,1)S(1)} collective-permute-done((bf16[8,128,128]{2,1,0:T(8,128)(2,1)S(1)}, bf16[8,128,128]{2,1,0:T(8,128)(2,1)S(1)}, u32[]{:S(2)}, u32[]{:S(2)}) %collective-permute-start.4) | collective-permute-done | bytes 262176 | tf_op jit(solution)/shard_map/ppermute | solution.py:133
  82.0 1.5 %fusion.59 = (f32[512]{0:T(512)S(1)}, f32[1,512,1,128]{3,1,2,0:T(8,128)S(1)}) fusion(f32[1,512,1,128]{3,1,2,0:T(8,128)} %fusion.15, f32[512]{0:T(512)S(1)} %exp.53, bf16[512,512]{1,0:T(8,128)(2,1)} %copy-done, f32[128,128]{1,0:T(8,128)S(1)} %multiply_reduce_fusion, f32[]{:T(128)} %bitcast.11), kind=kOutput, calls=%fused_computation.96 | convolution fusion | flops 100941312 | bytes 725504 | tf_op jit(solution)/shard_map/cthd,chde->cthe/dot_general | solution.py:106
  83.8 1.2 %fusion.32 = bf16[512,128]{1,0:T(8,128)(2,1)S(1)} fusion(f32[1,512,1,128]{3,1,2,0:T(8,128)S(1)} %get-tuple-element.46, f32[512,512]{1,0:T(8,128)} %get-tuple-element.44, f32[512]{0:T(512)S(1)} %add_sqrt_fusion, f32[512]{0:T(512)S(1)} %broadcast_multiply_fusion), kind=kLoop, calls=%fused_computation.43 | loop fusion | flops 524288 | bytes 659456 | tf_op jit(solution)/shard_map/convert_element_type | solution.py:113
  85.0 1.9 %collective-permute-start = (bf16[4,32,128]{2,1,0:T(8,128)(2,1)S(1)}, bf16[4,32,128]{2,1,0:T(8,128)(2,1)S(1)}, u32[]{:S(2)}, u32[]{:S(2)}) collective-permute-start(bf16[4,32,128]{2,1,0:T(8,128)(2,1)S(1)} %get-tuple-element.42), channel_id=1, source_target_pairs={{0,2},{1,3},{2,0},{3,1},{4,6},{5,7},{6,4},{7,5},{8,10},{9,11},{10,... | collective-permute-start | bytes 98312 | tf_op jit(solution)/shard_map/ppermute | solution.py:132
  86.9 1.8 %collective-permute-start.1 = (bf16[4,32,128]{2,1,0:T(8,128)(2,1)S(1)}, bf16[4,32,128]{2,1,0:T(8,128)(2,1)S(1)}, u32[]{:S(2)}, u32[]{:S(2)}) collective-permute-start(bf16[4,32,128]{2,1,0:T(8,128)(2,1)S(1)} %get-tuple-element.41), channel_id=1, source_target_pairs={{0,1},{1,2},{2,3},{3,0},{4,5},{5,6},{6,7},{7,4},{8,9},{9,10},{10,1... | collective-permute-start | bytes 98312 | tf_op jit(solution)/shard_map/ppermute | solution.py:132
  89.0 1.5 %collective-permute-done = bf16[4,32,128]{2,1,0:T(8,128)(2,1)S(1)} collective-permute-done((bf16[4,32,128]{2,1,0:T(8,128)(2,1)S(1)}, bf16[4,32,128]{2,1,0:T(8,128)(2,1)S(1)}, u32[]{:S(2)}, u32[]{:S(2)}) %collective-permute-start) | collective-permute-done | bytes 32800 | tf_op jit(solution)/shard_map/ppermute | solution.py:132
  90.8 3.0 %collective-permute-done.2 = bf16[4,32,128]{2,1,0:T(8,128)(2,1)S(1)} collective-permute-done((bf16[4,32,128]{2,1,0:T(8,128)(2,1)S(1)}, bf16[4,32,128]{2,1,0:T(8,128)(2,1)S(1)}, u32[]{:S(2)}, u32[]{:S(2)}) %collective-permute-start.2) | collective-permute-done | bytes 32800 | tf_op jit(solution)/shard_map/ppermute | solution.py:132
  94.4 2.2 %collective-permute-start.7 = (bf16[32,2048]{1,0:T(8,128)(2,1)S(1)}, bf16[32,2048]{1,0:T(8,128)(2,1)S(1)}, u32[]{:S(2)}, u32[]{:S(2)}) collective-permute-start(bf16[32,2048]{1,0:T(8,128)(2,1)S(1)} %get-tuple-element.25), channel_id=1, source_target_pairs={{0,8},{1,9},{2,10},{3,11},{4,12},{5,13},{6,14},{7,15},{8,0},{9,1},... | collective-permute-start | bytes 393224 | tf_op jit(solution)/shard_map/ppermute | solution.py:151
  97.2 2.6 %collective-permute-start.9 = (bf16[32,2048]{1,0:T(8,128)(2,1)S(1)}, bf16[32,2048]{1,0:T(8,128)(2,1)S(1)}, u32[]{:S(2)}, u32[]{:S(2)}) collective-permute-start(bf16[32,2048]{1,0:T(8,128)(2,1)S(1)} %get-tuple-element.26), channel_id=1, source_target_pairs={{0,12},{1,13},{2,14},{3,15},{4,0},{5,1},{6,2},{7,3},{8,4},{9,5},{1... | collective-permute-start | bytes 393224 | tf_op jit(solution)/shard_map/ppermute | solution.py:151
  99.8 1.9 %collective-permute-done.7 = bf16[32,2048]{1,0:T(8,128)(2,1)S(1)} collective-permute-done((bf16[32,2048]{1,0:T(8,128)(2,1)S(1)}, bf16[32,2048]{1,0:T(8,128)(2,1)S(1)}, u32[]{:S(2)}, u32[]{:S(2)}) %collective-permute-start.7) | collective-permute-done | bytes 131104 | tf_op jit(solution)/shard_map/ppermute | solution.py:151
  101.7 1.4 %collective-permute-done.8 = bf16[32,2048]{1,0:T(8,128)(2,1)S(1)} collective-permute-done((bf16[32,2048]{1,0:T(8,128)(2,1)S(1)}, bf16[32,2048]{1,0:T(8,128)(2,1)S(1)}, u32[]{:S(2)}, u32[]{:S(2)}) %collective-permute-start.8) | collective-permute-done | bytes 131104 | tf_op jit(solution)/shard_map/ppermute | solution.py:151
  (51 shorter events, 8.8 us)
Async XLA Ops:
  6.5 46.1 %all-gather.2.cloned.1.call-start = ((), (), s32[]{:S(2)}) async-start(), calls=%async_computation.2 | async-start | bytes 2785280 | tf_op jit(solution)/shard_map/all_gather | solution.py:53
  10.6 7.6 %copy-start.1 = (f32[512,1]{0,1:T(1,128)S(1)}, f32[512,1]{0,1:T(1,128)}, u32[]{:S(2)}) copy-start(f32[512,1]{0,1:T(1,128)} %param.8) | copy-start | bytes 6148
  10.6 35.8 %all-to-all-start = ((bf16[16,32,2048]{2,1,0:T(8,128)(2,1)}), bf16[16,32,2048]{2,1,0:T(8,128)(2,1)S(1)}, u32[]{:S(2)}, u32[]{:S(2)}) async-start(bf16[16,32,2048]{2,1,0:T(8,128)(2,1)} %broadcast_in_dim.113), calls=%async_computation | async-start | bytes 4194304 | tf_op jit(solution)/shard_map/all_to_all | solution.py:14
  56.4 14.3 %copy-start = (bf16[512,512]{1,0:T(8,128)(2,1)}, bf16[512,512]{1,0:T(8,128)(2,1)S(1)}, u32[]{:S(2)}) copy-start(bf16[512,512]{1,0:T(8,128)(2,1)S(1)} %get-tuple-element.43) | copy-start | bytes 1572868
  57.8 23.7 %all-to-all-start.1 = ((bf16[16,1,136,128]{3,2,1,0:T(8,128)(2,1)}), bf16[16,1,136,128]{3,2,1,0:T(8,128)(2,1)S(1)}, u32[]{:S(2)}, u32[]{:S(2)}) async-start(bf16[16,1,136,128]{3,2,1,0:T(8,128)(2,1)} %broadcast_in_dim.122), calls=%async_computation.1 | async-start | bytes 1114112 | tf_op jit(solution)/shard_map/all_to_all | solution.py:14
  65.6 10.8 %collective-permute-start.3 = (bf16[8,128,128]{2,1,0:T(8,128)(2,1)S(1)}, bf16[8,128,128]{2,1,0:T(8,128)(2,1)S(1)}, u32[]{:S(2)}, u32[]{:S(2)}) collective-permute-start(bf16[8,128,128]{2,1,0:T(8,128)(2,1)S(1)} %constant_dynamic-slice_fusion), channel_id=1, source_target_pairs={{0,2},{1,3},{2,0},{3,1},{4,6},{5,7},{6,4},{7,5},{8,10},{9,11},{10,... | collective-permute-start | bytes 786440 | tf_op jit(solution)/shard_map/ppermute | solution.py:133
  67.1 13.4 %collective-permute-start.4 = (bf16[8,128,128]{2,1,0:T(8,128)(2,1)S(1)}, bf16[8,128,128]{2,1,0:T(8,128)(2,1)S(1)}, u32[]{:S(2)}, u32[]{:S(2)}) collective-permute-start(bf16[8,128,128]{2,1,0:T(8,128)(2,1)S(1)} %constant_dynamic-slice_fusion), channel_id=1, source_target_pairs={{0,1},{1,2},{2,3},{3,0},{4,5},{5,6},{6,7},{7,4},{8,9},{9,10},{10,1... | collective-permute-start | bytes 786440 | tf_op jit(solution)/shard_map/ppermute | solution.py:133
  69.5 11.8 %collective-permute-start.5 = (bf16[8,128,128]{2,1,0:T(8,128)(2,1)S(1)}, bf16[8,128,128]{2,1,0:T(8,128)(2,1)S(1)}, u32[]{:S(2)}, u32[]{:S(2)}) collective-permute-start(bf16[8,128,128]{2,1,0:T(8,128)(2,1)S(1)} %constant_dynamic-slice_fusion), channel_id=1, source_target_pairs={{0,3},{1,0},{2,1},{3,2},{4,7},{5,4},{6,5},{7,6},{8,11},{9,8},{10,9... | collective-permute-start | bytes 786440 | tf_op jit(solution)/shard_map/ppermute | solution.py:133
  81.3 7.5 %collective-permute-start.6 = (bf16[3,8,128,128]{3,2,0,1:T(8,128)(2,1)S(1)}, bf16[3,8,128,128]{3,2,0,1:T(8,128)(2,1)S(1)}, u32[]{:S(2)}, u32[]{:S(2)}) collective-permute-start(bf16[3,8,128,128]{3,2,0,1:T(8,128)(2,1)S(1)} %pad_maximum_fusion), channel_id=1, source_target_pairs={{0,16},{16,0},{32,48},{48,32},{64,80},{80,64},{96,112},{112,96},{1... | collective-permute-start | bytes 2359304 | tf_op jit(solution)/shard_map/ppermute | solution.py:135
  85.0 5.5 %collective-permute-start = (bf16[4,32,128]{2,1,0:T(8,128)(2,1)S(1)}, bf16[4,32,128]{2,1,0:T(8,128)(2,1)S(1)}, u32[]{:S(2)}, u32[]{:S(2)}) collective-permute-start(bf16[4,32,128]{2,1,0:T(8,128)(2,1)S(1)} %get-tuple-element.42), channel_id=1, source_target_pairs={{0,2},{1,3},{2,0},{3,1},{4,6},{5,7},{6,4},{7,5},{8,10},{9,11},{10,... | collective-permute-start | bytes 98312 | tf_op jit(solution)/shard_map/ppermute | solution.py:132
  86.9 3.9 %collective-permute-start.1 = (bf16[4,32,128]{2,1,0:T(8,128)(2,1)S(1)}, bf16[4,32,128]{2,1,0:T(8,128)(2,1)S(1)}, u32[]{:S(2)}, u32[]{:S(2)}) collective-permute-start(bf16[4,32,128]{2,1,0:T(8,128)(2,1)S(1)} %get-tuple-element.41), channel_id=1, source_target_pairs={{0,1},{1,2},{2,3},{3,0},{4,5},{5,6},{6,7},{7,4},{8,9},{9,10},{10,1... | collective-permute-start | bytes 98312 | tf_op jit(solution)/shard_map/ppermute | solution.py:132
  88.7 5.1 %collective-permute-start.2 = (bf16[4,32,128]{2,1,0:T(8,128)(2,1)S(1)}, bf16[4,32,128]{2,1,0:T(8,128)(2,1)S(1)}, u32[]{:S(2)}, u32[]{:S(2)}) collective-permute-start(bf16[4,32,128]{2,1,0:T(8,128)(2,1)S(1)} %get-tuple-element.40), channel_id=1, source_target_pairs={{0,3},{1,0},{2,1},{3,2},{4,7},{5,4},{6,5},{7,6},{8,11},{9,8},{10,9... | collective-permute-start | bytes 98312 | tf_op jit(solution)/shard_map/ppermute | solution.py:132
  94.4 7.3 %collective-permute-start.7 = (bf16[32,2048]{1,0:T(8,128)(2,1)S(1)}, bf16[32,2048]{1,0:T(8,128)(2,1)S(1)}, u32[]{:S(2)}, u32[]{:S(2)}) collective-permute-start(bf16[32,2048]{1,0:T(8,128)(2,1)S(1)} %get-tuple-element.25), channel_id=1, source_target_pairs={{0,8},{1,9},{2,10},{3,11},{4,12},{5,13},{6,14},{7,15},{8,0},{9,1},... | collective-permute-start | bytes 393224 | tf_op jit(solution)/shard_map/ppermute | solution.py:151
  96.6 6.5 %collective-permute-start.8 = (bf16[32,2048]{1,0:T(8,128)(2,1)S(1)}, bf16[32,2048]{1,0:T(8,128)(2,1)S(1)}, u32[]{:S(2)}, u32[]{:S(2)}) collective-permute-start(bf16[32,2048]{1,0:T(8,128)(2,1)S(1)} %get-tuple-element.36), channel_id=1, source_target_pairs={{0,4},{1,5},{2,6},{3,7},{4,8},{5,9},{6,10},{7,11},{8,12},{9,13},{1... | collective-permute-start | bytes 393224 | tf_op jit(solution)/shard_map/ppermute | solution.py:151
  97.2 5.9 %collective-permute-start.9 = (bf16[32,2048]{1,0:T(8,128)(2,1)S(1)}, bf16[32,2048]{1,0:T(8,128)(2,1)S(1)}, u32[]{:S(2)}, u32[]{:S(2)}) collective-permute-start(bf16[32,2048]{1,0:T(8,128)(2,1)S(1)} %get-tuple-element.26), channel_id=1, source_target_pairs={{0,12},{1,13},{2,14},{3,15},{4,0},{5,1},{6,2},{7,3},{8,4},{9,5},{1... | collective-permute-start | bytes 393224 | tf_op jit(solution)/shard_map/ppermute | solution.py:151
Sparse Core Ops, SparseCore 0:
  9.2 43.3 all-gather.1
where the time goes:
time: 111 us
  waiting for transfers between devices  47.6 us (43%)
  starting transfers between devices  24.9 us (22%)
  between operations  17.6 us (16%)
  matrix products  7.4 us (7%)
  local copies, waits for them, and re-layouts  7.38 us (7%)
  other arithmetic  5.77 us (5%)
    all_to_all x2, waiting for transfers between devices, gather_by_exchange(): return lax.all_to_all(copies, axis, 0, 0, tiled=False)  22.9 us
    all_to_all x2, starting transfers between devices, gather_by_exchange(): return lax.all_to_all(copies, axis, 0, 0, tiled=False)  11.6 us
    ppermute x3, waiting for transfers between devices, shards(): fetched.append(lax.ppermute(own_half, 'head', across))  10.5 us
    all_gather x1, waiting for transfers between devices, shards(): stacked = lax.all_gather(packed, 'tm', axis=0, tiled=True)  6.14 us
    ppermute x3, starting transfers between devices, shards(): total = total + lax.ppermute(piece, 'head', down).astype(jnp.float32)  5.39 us
    ppermute x3, waiting for transfers between devices, shards(): pieces.append(lax.ppermute(piece, 'head', across))  4.76 us
    ppermute x3, starting transfers between devices, shards(): pieces.append(lax.ppermute(piece, 'head', across))  3.92 us
    ppermute x3, starting transfers between devices, shards(): fetched.append(lax.ppermute(own_half, 'head', across))  3.91 us
  transfers between devices with their start and end apart: 13, of which 10 were waited for; matrix products, arithmetic and copies ran while one was open for 11% of the time, Pallas kernels for 0%

commit v1 on v0

--- a/solution.py
+++ b/solution.py
@@ -6,6 +6,17 @@
 HEAD_DIM = 128
 BLOCK = 512
 PAD_ROWS = 8
+
+
+def gather_by_hops(block, axis, along):
+    size = lax.axis_size(axis)
+    right = [(i, (i + 1) % size) for i in range(size)]
+    parts = [block]
+    for far in range(1, size):
+        parts = [lax.ppermute(parts[0], axis, right), *parts]
+    out = jnp.concatenate(parts, axis=along)
+    places = (lax.axis_index(axis) + 1) * parts[-1].shape[along]
+    return jnp.roll(out, places, axis=along)
 
 
 def gather_by_exchange(part, axis):
@@ -50,7 +61,7 @@
     for start, block in reversed(list(zip(range(0, width, head_width), blocks))[:-1]):
         padded = jnp.pad(block, ((0, 0), (start, width - start - head_width)))
         packed = jnp.where(column < start + head_width, padded, packed)
-    stacked = lax.all_gather(packed, "tm", axis=0, tiled=True)
+    stacked = gather_by_hops(packed, "tm", 0)
     joined = stacked[:, : 4 * head_width]
     out_blocks = stacked[:, 4 * head_width :].reshape(-1, head_width, w_out.shape[1])
     frames_here = gather_by_exchange(frames, "head").reshape(-1, frames.shape[1])

time: 111 us -> 187 us (1.68)
  waiting for transfers between devices: 47.6 us -> 99.4 us
  local copies, waits for them, and re-layouts: 7.38 us -> 41.9 us
  between operations: 17.6 us -> 4.22 us
  starting transfers between devices: 24.9 us -> 27.3 us
    ppermute x0 -> x15, waiting for transfers between devices: none -> 82.3 us  [gather_by_hops(): parts = [lax.ppermute(parts[0], axis, right), *parts]]
    unnamed x4 -> x51, local copies, waits for them, and re-layouts: 0.01 us -> 33.7 us
    all_to_all x2, waiting for transfers between devices: 22.9 us -> 0.01 us  [gather_by_exchange(): return lax.all_to_all(copies, axis, 0, 0, tiled=False)]
    all_gather x1 -> x0, waiting for transfers between devices: 6.14 us -> none  [shards(): stacked = lax.all_gather(packed, 'tm', axis=0, tiled=True)]
    all_to_all x2, starting transfers between devices: 11.6 us -> 13.6 us  [gather_by_exchange(): return lax.all_to_all(copies, axis, 0, 0, tiled=False)]
  transfers between devices with their start and end apart: 13 -> 27, of which waited for: 10 -> 21; matrix products, arithmetic and copies ran while one was open for 11% -> 24% of each run, Pallas kernels for 0% -> 0%
where the time goes in v1:
time: 187 us; the launch traced here: 186 us
  waiting for transfers between devices  99.4 us (53%)
  local copies, waits for them, and re-layouts  41.9 us (22%)
  starting transfers between devices  27.3 us (15%)
  matrix products  8.46 us (5%)
  other arithmetic  5.04 us (3%)
  between operations  4.22 us (2%)
    ppermute x15, waiting for transfers between devices, gather_by_hops(): parts = [lax.ppermute(parts[0], axis, right), *parts]  82.3 us
    unnamed x51, local copies, waits for them, and re-layouts  33.7 us
    all_to_all x2, starting transfers between devices, gather_by_exchange(): return lax.all_to_all(copies, axis, 0, 0, tiled=False)  13.6 us
    ppermute x3, waiting for transfers between devices, shards(): fetched.append(lax.ppermute(own_half, 'head', across))  9.78 us
    ppermute x3, starting transfers between devices, shards(): total = total + lax.ppermute(piece, 'head', down).astype(jnp.float32)  6.3 us
    ppermute x3, waiting for transfers between devices, shards(): pieces.append(lax.ppermute(piece, 'head', across))  4.12 us
    dot_general x1, matrix products, shards(): projected = jnp.dot(frames_here, joined, preferred_element_type=jnp.float32)  3.85 us
  transfers between devices with their start and end apart: 27, of which 21 were waited for; matrix products, arithmetic and copies ran while one was open for 24% of the time, Pallas kernels for 0%

profile of v1, /device:TPU:6, one launch (start us, length us, event | category | flops | bytes accessed | tf_op | source)
XLA Modules:
  0.0 186.3 jit_solution(2089214980598497506)
XLA Ops:
  0.9 8.3 %collective-permute-done = bf16[128,640]{1,0:T(8,128)(2,1)S(1)} collective-permute-done((bf16[128,640]{1,0:T(8,128)(2,1)S(1)}, bf16[128,640]{1,0:T(8,128)(2,1)S(1)}, u32[]{:S(2)}, u32[]{:S(2)}) %collective-permute-start) | collective-permute-done | bytes 163872 | tf_op jit(solution)/shard_map/ppermute | solution.py:16
  9.2 6.0 %collective-permute-done.1 = bf16[128,640]{1,0:T(8,128)(2,1)S(1)} collective-permute-done((bf16[128,640]{1,0:T(8,128)(2,1)S(1)}, bf16[128,640]{1,0:T(8,128)(2,1)S(1)}, u32[]{:S(2)}, u32[]{:S(2)}) %collective-permute-start.1) | collective-permute-done | bytes 163872 | tf_op jit(solution)/shard_map/ppermute | solution.py:16
  15.2 6.0 %collective-permute-done.2 = bf16[128,640]{1,0:T(8,128)(2,1)S(1)} collective-permute-done((bf16[128,640]{1,0:T(8,128)(2,1)S(1)}, bf16[128,640]{1,0:T(8,128)(2,1)S(1)}, u32[]{:S(2)}, u32[]{:S(2)}) %collective-permute-start.2) | collective-permute-done | bytes 163872 | tf_op jit(solution)/shard_map/ppermute | solution.py:16
  21.1 6.0 %collective-permute-done.3 = bf16[128,640]{1,0:T(8,128)(2,1)S(1)} collective-permute-done((bf16[128,640]{1,0:T(8,128)(2,1)S(1)}, bf16[128,640]{1,0:T(8,128)(2,1)S(1)}, u32[]{:S(2)}, u32[]{:S(2)}) %collective-permute-start.3) | collective-permute-done | bytes 163872 | tf_op jit(solution)/shard_map/ppermute | solution.py:16
  27.1 6.0 %collective-permute-done.4 = bf16[128,640]{1,0:T(8,128)(2,1)S(1)} collective-permute-done((bf16[128,640]{1,0:T(8,128)(2,1)S(1)}, bf16[128,640]{1,0:T(8,128)(2,1)S(1)}, u32[]{:S(2)}, u32[]{:S(2)}) %collective-permute-start.4) | collective-permute-done | bytes 163872 | tf_op jit(solution)/shard_map/ppermute | solution.py:16
  33.0 6.0 %collective-permute-done.5 = bf16[128,640]{1,0:T(8,128)(2,1)S(1)} collective-permute-done((bf16[128,640]{1,0:T(8,128)(2,1)S(1)}, bf16[128,640]{1,0:T(8,128)(2,1)S(1)}, u32[]{:S(2)}, u32[]{:S(2)}) %collective-permute-start.5) | collective-permute-done | bytes 163872 | tf_op jit(solution)/shard_map/ppermute | solution.py:16
  39.0 6.0 %collective-permute-done.6 = bf16[128,640]{1,0:T(8,128)(2,1)S(1)} collective-permute-done((bf16[128,640]{1,0:T(8,128)(2,1)S(1)}, bf16[128,640]{1,0:T(8,128)(2,1)S(1)}, u32[]{:S(2)}, u32[]{:S(2)}) %collective-permute-start.6) | collective-permute-done | bytes 163872 | tf_op jit(solution)/shard_map/ppermute | solution.py:16
  45.0 6.0 %collective-permute-done.7 = bf16[128,640]{1,0:T(8,128)(2,1)S(1)} collective-permute-done((bf16[128,640]{1,0:T(8,128)(2,1)S(1)}, bf16[128,640]{1,0:T(8,128)(2,1)S(1)}, u32[]{:S(2)}, u32[]{:S(2)}) %collective-permute-start.7) | collective-permute-done | bytes 163872 | tf_op jit(solution)/shard_map/ppermute | solution.py:16
  51.6 6.0 %collective-permute-done.8 = bf16[128,640]{1,0:T(8,128)(2,1)S(1)} collective-permute-done((bf16[128,640]{1,0:T(8,128)(2,1)S(1)}, bf16[128,640]{1,0:T(8,128)(2,1)S(1)}, u32[]{:S(2)}, u32[]{:S(2)}) %collective-permute-start.8) | collective-permute-done | bytes 163872 | tf_op jit(solution)/shard_map/ppermute | solution.py:16
  58.2 6.0 %collective-permute-done.9 = bf16[128,640]{1,0:T(8,128)(2,1)S(1)} collective-permute-done((bf16[128,640]{1,0:T(8,128)(2,1)S(1)}, bf16[128,640]{1,0:T(8,128)(2,1)S(1)}, u32[]{:S(2)}, u32[]{:S(2)}) %collective-permute-start.9) | collective-permute-done | bytes 163872 | tf_op jit(solution)/shard_map/ppermute | solution.py:16
  64.8 6.0 %collective-permute-done.10 = bf16[128,640]{1,0:T(8,128)(2,1)S(1)} collective-permute-done((bf16[128,640]{1,0:T(8,128)(2,1)S(1)}, bf16[128,640]{1,0:T(8,128)(2,1)S(1)}, u32[]{:S(2)}, u32[]{:S(2)}) %collective-permute-start.10) | collective-permute-done | bytes 163872 | tf_op jit(solution)/shard_map/ppermute | solution.py:16
  71.4 6.1 %collective-permute-done.11 = bf16[128,640]{1,0:T(8,128)(2,1)} collective-permute-done((bf16[128,640]{1,0:T(8,128)(2,1)S(1)}, bf16[128,640]{1,0:T(8,128)(2,1)}, u32[]{:S(2)}, u32[]{:S(2)}) %collective-permute-start.11) | collective-permute-done | bytes 163872 | tf_op jit(solution)/shard_map/ppermute | solution.py:16
  77.5 2.5 %broadcast_in_dim.113 = bf16[16,32,2048]{2,1,0:T(8,128)(2,1)} broadcast(bf16[32,2048]{1,0:T(8,128)(2,1)} %param.7), dimensions={1,2} | broadcast | bytes 2228224 | tf_op jit(solution)/shard_map/broadcast_in_dim | solution.py:24
  80.0 7.4 %all-to-all-start = ((bf16[16,32,2048]{2,1,0:T(8,128)(2,1)}), bf16[16,32,2048]{2,1,0:T(8,128)(2,1)S(1)}, u32[]{:S(2)}, u32[]{:S(2)}) async-start(bf16[16,32,2048]{2,1,0:T(8,128)(2,1)} %broadcast_in_dim.113), calls=%async_computation | async-start | bytes 4194304 | tf_op jit(solution)/shard_map/all_to_all | solution.py:25
  92.6 2.4 %collective-permute-done.13 = bf16[128,640]{1,0:T(8,128)(2,1)} collective-permute-done((bf16[128,640]{1,0:T(8,128)(2,1)}, bf16[128,640]{1,0:T(8,128)(2,1)}, u32[]{:S(2)}, u32[]{:S(2)}) %collective-permute-start.13) | collective-permute-done | bytes 163872 | tf_op jit(solution)/shard_map/ppermute | solution.py:16
  95.1 6.1 %collective-permute-done.14 = bf16[128,640]{1,0:T(8,128)(2,1)S(1)} collective-permute-done((bf16[128,640]{1,0:T(8,128)(2,1)}, bf16[128,640]{1,0:T(8,128)(2,1)S(1)}, u32[]{:S(2)}, u32[]{:S(2)}) %collective-permute-start.14) | collective-permute-done | bytes 163872 | tf_op jit(solution)/shard_map/ppermute | solution.py:16
  132.1 3.9 %fusion.59 = (bf16[512,512]{1,0:T(8,128)(2,1)S(1)}, f32[512,512]{1,0:T(8,128)}) fusion(bf16[512,2048]{1,0:T(8,128)(2,1)S(1)} %bitcast.110, bf16[4096,640]{1,0:T(8,128)(2,1)} %constant_dynamic-update-slice_fusion, s32[]{:T(128)S(6)} %select_n.138), kind=kOutput, calls=%fused_computation.128 | convolution fusion | flops 1074003968 | bytes 5767172 | tf_op jit(solution)/shard_map/dot_general | solution.py:68
  138.1 6.2 %all-to-all-start.1 = ((bf16[16,1,136,128]{3,2,1,0:T(8,128)(2,1)}), bf16[16,1,136,128]{3,2,1,0:T(8,128)(2,1)S(1)}, u32[]{:S(2)}, u32[]{:S(2)}) async-start(bf16[16,1,136,128]{3,2,1,0:T(8,128)(2,1)} %broadcast_in_dim.122), calls=%async_computation.1 | async-start | bytes 1114112 | tf_op jit(solution)/shard_map/all_to_all | solution.py:25
  154.2 4.9 %collective-permute-done.18 = bf16[8,128,128]{2,1,0:T(8,128)(2,1)S(1)} collective-permute-done((bf16[8,128,128]{2,1,0:T(8,128)(2,1)S(1)}, bf16[8,128,128]{2,1,0:T(8,128)(2,1)S(1)}, u32[]{:S(2)}, u32[]{:S(2)}) %collective-permute-start.18) | collective-permute-done | bytes 262176 | tf_op jit(solution)/shard_map/ppermute | solution.py:144
  159.0 2.6 %collective-permute-done.19 = bf16[8,128,128]{2,1,0:T(8,128)(2,1)S(1)} collective-permute-done((bf16[8,128,128]{2,1,0:T(8,128)(2,1)S(1)}, bf16[8,128,128]{2,1,0:T(8,128)(2,1)S(1)}, u32[]{:S(2)}, u32[]{:S(2)}) %collective-permute-start.19) | collective-permute-done | bytes 262176 | tf_op jit(solution)/shard_map/ppermute | solution.py:144
  161.6 2.3 %collective-permute-done.20 = bf16[8,128,128]{2,1,0:T(8,128)(2,1)S(1)} collective-permute-done((bf16[8,128,128]{2,1,0:T(8,128)(2,1)S(1)}, bf16[8,128,128]{2,1,0:T(8,128)(2,1)S(1)}, u32[]{:S(2)}, u32[]{:S(2)}) %collective-permute-start.20) | collective-permute-done | bytes 262176 | tf_op jit(solution)/shard_map/ppermute | solution.py:144
  173.2 2.4 %collective-permute-done.17 = bf16[4,32,128]{2,1,0:T(8,128)(2,1)S(1)} collective-permute-done((bf16[4,32,128]{2,1,0:T(8,128)(2,1)S(1)}, bf16[4,32,128]{2,1,0:T(8,128)(2,1)S(1)}, u32[]{:S(2)}, u32[]{:S(2)}) %collective-permute-start.17) | collective-permute-done | bytes 32800 | tf_op jit(solution)/shard_map/ppermute | solution.py:143
  176.2 3.1 %collective-permute-start.22 = (bf16[32,2048]{1,0:T(8,128)(2,1)S(1)}, bf16[32,2048]{1,0:T(8,128)(2,1)S(1)}, u32[]{:S(2)}, u32[]{:S(2)}) collective-permute-start(bf16[32,2048]{1,0:T(8,128)(2,1)S(1)} %get-tuple-element.25), channel_id=1, source_target_pairs={{0,8},{1,9},{2,10},{3,11},{4,12},{5,13},{6,14},{7,15},{8,0},{9,1},... | collective-permute-start | bytes 393224 | tf_op jit(solution)/shard_map/ppermute | solution.py:162
  179.8 2.7 %collective-permute-start.24 = (bf16[32,2048]{1,0:T(8,128)(2,1)S(1)}, bf16[32,2048]{1,0:T(8,128)(2,1)S(1)}, u32[]{:S(2)}, u32[]{:S(2)}) collective-permute-start(bf16[32,2048]{1,0:T(8,128)(2,1)S(1)} %get-tuple-element.26), channel_id=1, source_target_pairs={{0,12},{1,13},{2,14},{3,15},{4,0},{5,1},{6,2},{7,3},{8,4},{9,5},{1... | collective-permute-start | bytes 393224 | tf_op jit(solution)/shard_map/ppermute | solution.py:162
  (126 shorter events, 61.9 us)
Async XLA Ops:
  0.9 8.3 %collective-permute-start = (bf16[128,640]{1,0:T(8,128)(2,1)S(1)}, bf16[128,640]{1,0:T(8,128)(2,1)S(1)}, u32[]{:S(2)}, u32[]{:S(2)}) collective-permute-start(bf16[128,640]{1,0:T(8,128)(2,1)S(1)} %select_select_fusion), channel_id=1, source_target_pairs={{0,16},{16,32},{32,48},{48,64},{64,80},{80,96},{96,112},{112,128},... | collective-permute-start | bytes 491528 | tf_op jit(solution)/shard_map/ppermute | solution.py:16
  9.2 6.0 %collective-permute-start.1 = (bf16[128,640]{1,0:T(8,128)(2,1)S(1)}, bf16[128,640]{1,0:T(8,128)(2,1)S(1)}, u32[]{:S(2)}, u32[]{:S(2)}) collective-permute-start(bf16[128,640]{1,0:T(8,128)(2,1)S(1)} %collective-permute-done), channel_id=1, source_target_pairs={{0,16},{16,32},{32,48},{48,64},{64,80},{80,96},{96,112},{112,128},... | collective-permute-start | bytes 491528 | tf_op jit(solution)/shard_map/ppermute | solution.py:16
  15.2 6.0 %collective-permute-start.2 = (bf16[128,640]{1,0:T(8,128)(2,1)S(1)}, bf16[128,640]{1,0:T(8,128)(2,1)S(1)}, u32[]{:S(2)}, u32[]{:S(2)}) collective-permute-start(bf16[128,640]{1,0:T(8,128)(2,1)S(1)} %collective-permute-done.1), channel_id=1, source_target_pairs={{0,16},{16,32},{32,48},{48,64},{64,80},{80,96},{96,112},{112,128},... | collective-permute-start | bytes 491528 | tf_op jit(solution)/shard_map/ppermute | solution.py:16
  21.1 6.0 %collective-permute-start.3 = (bf16[128,640]{1,0:T(8,128)(2,1)S(1)}, bf16[128,640]{1,0:T(8,128)(2,1)S(1)}, u32[]{:S(2)}, u32[]{:S(2)}) collective-permute-start(bf16[128,640]{1,0:T(8,128)(2,1)S(1)} %collective-permute-done.2), channel_id=1, source_target_pairs={{0,16},{16,32},{32,48},{48,64},{64,80},{80,96},{96,112},{112,128},... | collective-permute-start | bytes 491528 | tf_op jit(solution)/shard_map/ppermute | solution.py:16
  27.1 6.0 %collective-permute-start.4 = (bf16[128,640]{1,0:T(8,128)(2,1)S(1)}, bf16[128,640]{1,0:T(8,128)(2,1)S(1)}, u32[]{:S(2)}, u32[]{:S(2)}) collective-permute-start(bf16[128,640]{1,0:T(8,128)(2,1)S(1)} %collective-permute-done.3), channel_id=1, source_target_pairs={{0,16},{16,32},{32,48},{48,64},{64,80},{80,96},{96,112},{112,128},... | collective-permute-start | bytes 491528 | tf_op jit(solution)/shard_map/ppermute | solution.py:16
  33.0 6.0 %collective-permute-start.5 = (bf16[128,640]{1,0:T(8,128)(2,1)S(1)}, bf16[128,640]{1,0:T(8,128)(2,1)S(1)}, u32[]{:S(2)}, u32[]{:S(2)}) collective-permute-start(bf16[128,640]{1,0:T(8,128)(2,1)S(1)} %collective-permute-done.4), channel_id=1, source_target_pairs={{0,16},{16,32},{32,48},{48,64},{64,80},{80,96},{96,112},{112,128},... | collective-permute-start | bytes 491528 | tf_op jit(solution)/shard_map/ppermute | solution.py:16
  39.0 6.0 %collective-permute-start.6 = (bf16[128,640]{1,0:T(8,128)(2,1)S(1)}, bf16[128,640]{1,0:T(8,128)(2,1)S(1)}, u32[]{:S(2)}, u32[]{:S(2)}) collective-permute-start(bf16[128,640]{1,0:T(8,128)(2,1)S(1)} %collective-permute-done.5), channel_id=1, source_target_pairs={{0,16},{16,32},{32,48},{48,64},{64,80},{80,96},{96,112},{112,128},... | collective-permute-start | bytes 491528 | tf_op jit(solution)/shard_map/ppermute | solution.py:16
  45.0 6.0 %collective-permute-start.7 = (bf16[128,640]{1,0:T(8,128)(2,1)S(1)}, bf16[128,640]{1,0:T(8,128)(2,1)S(1)}, u32[]{:S(2)}, u32[]{:S(2)}) collective-permute-start(bf16[128,640]{1,0:T(8,128)(2,1)S(1)} %collective-permute-done.6), channel_id=1, source_target_pairs={{0,16},{16,32},{32,48},{48,64},{64,80},{80,96},{96,112},{112,128},... | collective-permute-start | bytes 491528 | tf_op jit(solution)/shard_map/ppermute | solution.py:16
  51.6 6.0 %collective-permute-start.8 = (bf16[128,640]{1,0:T(8,128)(2,1)S(1)}, bf16[128,640]{1,0:T(8,128)(2,1)S(1)}, u32[]{:S(2)}, u32[]{:S(2)}) collective-permute-start(bf16[128,640]{1,0:T(8,128)(2,1)S(1)} %collective-permute-done.7), channel_id=1, source_target_pairs={{0,16},{16,32},{32,48},{48,64},{64,80},{80,96},{96,112},{112,128},... | collective-permute-start | bytes 491528 | tf_op jit(solution)/shard_map/ppermute | solution.py:16
  58.2 6.0 %collective-permute-start.9 = (bf16[128,640]{1,0:T(8,128)(2,1)S(1)}, bf16[128,640]{1,0:T(8,128)(2,1)S(1)}, u32[]{:S(2)}, u32[]{:S(2)}) collective-permute-start(bf16[128,640]{1,0:T(8,128)(2,1)S(1)} %collective-permute-done.8), channel_id=1, source_target_pairs={{0,16},{16,32},{32,48},{48,64},{64,80},{80,96},{96,112},{112,128},... | collective-permute-start | bytes 491528 | tf_op jit(solution)/shard_map/ppermute | solution.py:16
  64.8 6.0 %collective-permute-start.10 = (bf16[128,640]{1,0:T(8,128)(2,1)S(1)}, bf16[128,640]{1,0:T(8,128)(2,1)S(1)}, u32[]{:S(2)}, u32[]{:S(2)}) collective-permute-start(bf16[128,640]{1,0:T(8,128)(2,1)S(1)} %collective-permute-done.9), channel_id=1, source_target_pairs={{0,16},{16,32},{32,48},{48,64},{64,80},{80,96},{96,112},{112,128},... | collective-permute-start | bytes 491528 | tf_op jit(solution)/shard_map/ppermute | solution.py:16
  71.4 6.1 %collective-permute-start.11 = (bf16[128,640]{1,0:T(8,128)(2,1)S(1)}, bf16[128,640]{1,0:T(8,128)(2,1)}, u32[]{:S(2)}, u32[]{:S(2)}) collective-permute-start(bf16[128,640]{1,0:T(8,128)(2,1)S(1)} %collective-permute-done.10), channel_id=1, source_target_pairs={{0,16},{16,32},{32,48},{48,64},{64,80},{80,96},{96,112},{112,128},... | collective-permute-start | bytes 491528 | tf_op jit(solution)/shard_map/ppermute | solution.py:16
  77.5 11.2 %collective-permute-start.12 = (bf16[128,640]{1,0:T(8,128)(2,1)}, bf16[128,640]{1,0:T(8,128)(2,1)}, u32[]{:S(2)}, u32[]{:S(2)}) collective-permute-start(bf16[128,640]{1,0:T(8,128)(2,1)} %collective-permute-done.11), channel_id=1, source_target_pairs={{0,16},{16,32},{32,48},{48,64},{64,80},{80,96},{96,112},{112,128},... | collective-permute-start | bytes 491528 | tf_op jit(solution)/shard_map/ppermute | solution.py:16
  80.0 52.1 %all-to-all-start = ((bf16[16,32,2048]{2,1,0:T(8,128)(2,1)}), bf16[16,32,2048]{2,1,0:T(8,128)(2,1)S(1)}, u32[]{:S(2)}, u32[]{:S(2)}) async-start(bf16[16,32,2048]{2,1,0:T(8,128)(2,1)} %broadcast_in_dim.113), calls=%async_computation | async-start | bytes 4194304 | tf_op jit(solution)/shard_map/all_to_all | solution.py:25
  88.7 6.3 %collective-permute-start.13 = (bf16[128,640]{1,0:T(8,128)(2,1)}, bf16[128,640]{1,0:T(8,128)(2,1)}, u32[]{:S(2)}, u32[]{:S(2)}) collective-permute-start(bf16[128,640]{1,0:T(8,128)(2,1)} %collective-permute-done.12), channel_id=1, source_target_pairs={{0,16},{16,32},{32,48},{48,64},{64,80},{80,96},{96,112},{112,128},... | collective-permute-start | bytes 491528 | tf_op jit(solution)/shard_map/ppermute | solution.py:16
  95.0 6.2 %collective-permute-start.14 = (bf16[128,640]{1,0:T(8,128)(2,1)}, bf16[128,640]{1,0:T(8,128)(2,1)S(1)}, u32[]{:S(2)}, u32[]{:S(2)}) collective-permute-start(bf16[128,640]{1,0:T(8,128)(2,1)} %collective-permute-done.13), channel_id=1, source_target_pairs={{0,16},{16,32},{32,48},{48,64},{64,80},{80,96},{96,112},{112,128},... | collective-permute-start | bytes 491528 | tf_op jit(solution)/shard_map/ppermute | solution.py:16
  138.1 26.0 %all-to-all-start.1 = ((bf16[16,1,136,128]{3,2,1,0:T(8,128)(2,1)}), bf16[16,1,136,128]{3,2,1,0:T(8,128)(2,1)S(1)}, u32[]{:S(2)}, u32[]{:S(2)}) async-start(bf16[16,1,136,128]{3,2,1,0:T(8,128)(2,1)} %broadcast_in_dim.122), calls=%async_computation.1 | async-start | bytes 1114112 | tf_op jit(solution)/shard_map/all_to_all | solution.py:25
  148.3 10.8 %collective-permute-start.18 = (bf16[8,128,128]{2,1,0:T(8,128)(2,1)S(1)}, bf16[8,128,128]{2,1,0:T(8,128)(2,1)S(1)}, u32[]{:S(2)}, u32[]{:S(2)}) collective-permute-start(bf16[8,128,128]{2,1,0:T(8,128)(2,1)S(1)} %constant_dynamic-slice_fusion), channel_id=1, source_target_pairs={{0,2},{1,3},{2,0},{3,1},{4,6},{5,7},{6,4},{7,5},{8,10},{9,11},{10,... | collective-permute-start | bytes 786440 | tf_op jit(solution)/shard_map/ppermute | solution.py:144
  149.8 11.8 %collective-permute-start.19 = (bf16[8,128,128]{2,1,0:T(8,128)(2,1)S(1)}, bf16[8,128,128]{2,1,0:T(8,128)(2,1)S(1)}, u32[]{:S(2)}, u32[]{:S(2)}) collective-permute-start(bf16[8,128,128]{2,1,0:T(8,128)(2,1)S(1)} %constant_dynamic-slice_fusion), channel_id=1, source_target_pairs={{0,1},{1,2},{2,3},{3,0},{4,5},{5,6},{6,7},{7,4},{8,9},{9,10},{10,1... | collective-permute-start | bytes 786440 | tf_op jit(solution)/shard_map/ppermute | solution.py:144
  151.9 12.1 %collective-permute-start.20 = (bf16[8,128,128]{2,1,0:T(8,128)(2,1)S(1)}, bf16[8,128,128]{2,1,0:T(8,128)(2,1)S(1)}, u32[]{:S(2)}, u32[]{:S(2)}) collective-permute-start(bf16[8,128,128]{2,1,0:T(8,128)(2,1)S(1)} %constant_dynamic-slice_fusion), channel_id=1, source_target_pairs={{0,3},{1,0},{2,1},{3,2},{4,7},{5,4},{6,5},{7,6},{8,11},{9,8},{10,9... | collective-permute-start | bytes 786440 | tf_op jit(solution)/shard_map/ppermute | solution.py:144
  164.0 7.2 %collective-permute-start.21 = (bf16[3,8,128,128]{3,2,0,1:T(8,128)(2,1)S(1)}, bf16[3,8,128,128]{3,2,0,1:T(8,128)(2,1)S(1)}, u32[]{:S(2)}, u32[]{:S(2)}) collective-permute-start(bf16[3,8,128,128]{3,2,0,1:T(8,128)(2,1)S(1)} %pad_maximum_fusion), channel_id=1, source_target_pairs={{0,16},{16,0},{32,48},{48,32},{64,80},{80,64},{96,112},{112,96},{1... | collective-permute-start | bytes 2359304 | tf_op jit(solution)/shard_map/ppermute | solution.py:146
  176.2 7.7 %collective-permute-start.22 = (bf16[32,2048]{1,0:T(8,128)(2,1)S(1)}, bf16[32,2048]{1,0:T(8,128)(2,1)S(1)}, u32[]{:S(2)}, u32[]{:S(2)}) collective-permute-start(bf16[32,2048]{1,0:T(8,128)(2,1)S(1)} %get-tuple-element.25), channel_id=1, source_target_pairs={{0,8},{1,9},{2,10},{3,11},{4,12},{5,13},{6,14},{7,15},{8,0},{9,1},... | collective-permute-start | bytes 393224 | tf_op jit(solution)/shard_map/ppermute | solution.py:162
  179.2 6.4 %collective-permute-start.23 = (bf16[32,2048]{1,0:T(8,128)(2,1)S(1)}, bf16[32,2048]{1,0:T(8,128)(2,1)S(1)}, u32[]{:S(2)}, u32[]{:S(2)}) collective-permute-start(bf16[32,2048]{1,0:T(8,128)(2,1)S(1)} %get-tuple-element.36), channel_id=1, source_target_pairs={{0,4},{1,5},{2,6},{3,7},{4,8},{5,9},{6,10},{7,11},{8,12},{9,13},{1... | collective-permute-start | bytes 393224 | tf_op jit(solution)/shard_map/ppermute | solution.py:162
  179.8 5.8 %collective-permute-start.24 = (bf16[32,2048]{1,0:T(8,128)(2,1)S(1)}, bf16[32,2048]{1,0:T(8,128)(2,1)S(1)}, u32[]{:S(2)}, u32[]{:S(2)}) collective-permute-start(bf16[32,2048]{1,0:T(8,128)(2,1)S(1)} %get-tuple-element.26), channel_id=1, source_target_pairs={{0,12},{1,13},{2,14},{3,15},{4,0},{5,1},{6,2},{7,3},{8,4},{9,5},{1... | collective-permute-start | bytes 393224 | tf_op jit(solution)/shard_map/ppermute | solution.py:162
  (13 other events, 234.8 us)
